TPU v7x, 32 devices: a whole 2x2x4 slice. The times are simulated.
32 devices in a mesh: dp: 4 (over y, x), expert: 8 (over z, core).
Axes of the slice: x: 2, y: 2, z: 4, core: 2. Of those that a mesh axis runs over, the one named last changes fastest.
Arguments:
- tokens: bfloat16 [4096, 3584], P(('dp', 'expert')), may hold values from -6 to 6
- gate_probs: float32 [4096, 8], P(('dp', 'expert')), may hold values from 0.1 to 1
- expert_ids: int32 [4096, 8], P(('dp', 'expert')), may hold values from 0 to 63, all different within a row; in each aligned block of 128 rows (0 to 127, 128 to 255, ...) at most 24 rows name the same one
- cotangent: bfloat16 [4096, 3584], P(('dp', 'expert')), may hold values from -6 to 6
- w_gate: bfloat16 [8, 3584, 2048], P('expert', None, 'dp'), may hold values from -0.09375 to 0.09375
- w_up: bfloat16 [8, 3584, 2048], P('expert', None, 'dp'), may hold values from -0.09375 to 0.09375
- w_down: bfloat16 [8, 2048, 3584], P('expert', 'dp'), may hold values from -0.125 to 0.125
Outputs:
- layer_out: bfloat16 [4096, 3584], P(('dp', 'expert'))
- grad_tokens: bfloat16 [4096, 3584], P(('dp', 'expert'))
- grad_probs: float32 [4096, 8], P(('dp', 'expert'))
- grad_gate: bfloat16 [8, 3584, 2048], P('expert', None, 'dp')
- grad_up: bfloat16 [8, 3584, 2048], P('expert', None, 'dp')
- grad_down: bfloat16 [8, 2048, 3584], P('expert', 'dp')
Inputs may be any that keep to these rules, and one draw needn't show every extreme that they name: `expert_ids`: each token names 8 distinct ids. Among the 128 tokens of one device no id is named by more than 24 of them, a bound that some block reaches. Only ids below 8 belong to the window.
All inputs are finite; a program needn't handle non-finite values.
Results may differ from a plain program's by a relative error of at most 0.012.
Values may be sent and summed in bfloat16 or wider, within the bound.
No kernel may reach another device: no remote copies, remote signals or barrier semaphores. Data moves between devices by JAX's collectives and lax.ppermute only.
A program may use at most 192 MiB of HBM per device.

v0:
```python
import jax
import jax.numpy as jnp
from jax import lax
from jax.sharding import PartitionSpec as P


def slot_table(flat_ids, experts, capacity, sentinel):
    matches = (flat_ids[:, None] == jnp.arange(experts, dtype=jnp.int32)[None, :]).astype(jnp.int32)
    earlier = jnp.cumsum(matches, axis=0) - matches
    slot_pos = jnp.sum(earlier * matches, axis=1)
    target = jnp.where(flat_ids < experts, flat_ids * capacity + slot_pos, experts * capacity)
    flat_index = jnp.arange(flat_ids.shape[0], dtype=jnp.int32)
    blank_table = jnp.full((experts * capacity,), sentinel, jnp.int32)
    return blank_table.at[target].set(flat_index, mode="drop")


def contract_last(left, right):
    return lax.dot_general(
        left, right, (((1,), (1,)), ((), ())), preferred_element_type=jnp.float32
    )


def contract_first(left, right):
    return lax.dot_general(
        left, right, (((0,), (0,)), ((), ())), preferred_element_type=jnp.float32
    )


def dispatch(send_rows):
    along_expert = lax.all_to_all(send_rows, "expert", split_axis=0, concat_axis=0, tiled=True)
    return lax.all_gather(along_expert, "dp", axis=0, tiled=True)


def gather_back(partial_rows, groups):
    summed = lax.psum_scatter(partial_rows, "dp", scatter_dimension=0, tiled=True)
    return lax.all_to_all(summed, "expert", split_axis=0, concat_axis=0, tiled=True)


def expert_forward(rows_x, gate_w, up_w, down_w):
    gate_pre = jnp.dot(rows_x, gate_w, preferred_element_type=jnp.float32)
    up_pre = jnp.dot(rows_x, up_w, preferred_element_type=jnp.float32)
    hidden = (gate_pre * jax.nn.sigmoid(gate_pre) * up_pre).astype(jnp.bfloat16)
    part_out = jnp.dot(hidden, down_w, preferred_element_type=jnp.float32).astype(jnp.bfloat16)
    return lax.optimization_barrier((part_out, hidden, gate_pre, up_pre))


def expert_backward(rows_c, gate_pre, up_pre, gate_w, up_w, down_w):
    sigmoid_g = jax.nn.sigmoid(gate_pre)
    activated = gate_pre * sigmoid_g
    grad_hidden = contract_last(rows_c, down_w)
    grad_upin = (grad_hidden * activated).astype(jnp.bfloat16)
    grad_gatein = (grad_hidden * up_pre * sigmoid_g * (1.0 + gate_pre * (1.0 - sigmoid_g))).astype(
        jnp.bfloat16
    )
    part_dx = (contract_last(grad_gatein, gate_w) + contract_last(grad_upin, up_w)).astype(
        jnp.bfloat16
    )
    return (part_dx, grad_gatein, grad_upin)


def join_slots(chunks, experts, model_width):
    parts = [chunk.reshape(experts, -1, model_width) for chunk in chunks]
    return jnp.concatenate(parts, axis=1).reshape(-1, model_width)


def on_device(tokens, gate_probs, expert_ids, cotangent, w_gate, w_up, w_down):
    tok_count, model_width = tokens.shape
    top_k = expert_ids.shape[1]
    experts = lax.axis_size("expert")
    groups = lax.axis_size("dp")
    capacity = 3 * tok_count * top_k // (16 * experts)
    flat_count = tok_count * top_k
    slots = slot_table(expert_ids.reshape(-1), experts, capacity, flat_count)
    token_of = slots // top_k
    zero_row = jnp.zeros((1, model_width), jnp.bfloat16)
    send_x = jnp.concatenate([tokens, zero_row], 0)[token_of]
    rows_dy = jnp.concatenate([cotangent, zero_row], 0)[token_of]
    prob_rows = jnp.concatenate([gate_probs.reshape(-1), jnp.zeros((1,), jnp.float32)], 0)[slots]
    send_c = (prob_rows[:, None] * rows_dy.astype(jnp.float32)).astype(jnp.bfloat16)
    half = max(capacity // 2, 1)
    bounds = [(lo, hi) for lo, hi in ((0, half), (half, capacity)) if hi > lo]
    x_by_slot = send_x.reshape(experts, capacity, model_width)
    c_by_slot = send_c.reshape(experts, capacity, model_width)
    xs = [dispatch(x_by_slot[:, lo:hi].reshape(-1, model_width)) for lo, hi in bounds]
    cs = [dispatch(c_by_slot[:, lo:hi].reshape(-1, model_width)) for lo, hi in bounds]
    gate_w = w_gate[0]
    up_w = w_up[0]
    down_w = w_down[0]
    forwards = [expert_forward(rows_x, gate_w, up_w, down_w) for rows_x in xs]
    outs = [gather_back(fw[0], groups) for fw in forwards]
    backwards = [
        expert_backward(rows_c, fw[2], fw[3], gate_w, up_w, down_w)
        for rows_c, fw in zip(cs, forwards)
    ]
    dxs = [gather_back(bw[0], groups) for bw in backwards]
    new_gate = sum((contract_first(rx, bw[1]) for rx, bw in zip(xs, backwards)))
    new_up = sum((contract_first(rx, bw[2]) for rx, bw in zip(xs, backwards)))
    new_down = sum((contract_first(fw[1], rc) for fw, rc in zip(forwards, cs)))
    new_gate = new_gate.astype(jnp.bfloat16)[None]
    new_up = new_up.astype(jnp.bfloat16)[None]
    new_down = new_down.astype(jnp.bfloat16)[None]
    out_rows = join_slots(outs, experts, model_width).astype(jnp.float32)
    dx_rows = join_slots(dxs, experts, model_width).astype(jnp.float32)
    owner = (token_of[None, :] == jnp.arange(tok_count, dtype=jnp.int32)[:, None]).astype(
        jnp.float32
    )
    layer_out = jnp.dot(
        owner * prob_rows[None, :],
        out_rows,
        precision=lax.Precision.HIGHEST,
        preferred_element_type=jnp.float32,
    ).astype(jnp.bfloat16)
    grad_tokens = jnp.dot(
        owner, dx_rows, precision=lax.Precision.HIGHEST, preferred_element_type=jnp.float32
    ).astype(jnp.bfloat16)
    score_rows = jnp.sum(rows_dy.astype(jnp.float32) * out_rows, axis=1)
    grad_probs = (
        jnp.zeros((flat_count + 1,), jnp.float32)
        .at[slots]
        .set(score_rows)[:flat_count]
        .reshape(tok_count, top_k)
    )
    return (layer_out, grad_tokens, grad_probs, new_gate, new_up, new_down)


def solution(mesh):
    return jax.shard_map(
        on_device,
        mesh=mesh,
        in_specs=(
            P(("dp", "expert"), None),
            P(("dp", "expert"), None),
            P(("dp", "expert"), None),
            P(("dp", "expert"), None),
            P("expert", None, "dp"),
            P("expert", None, "dp"),
            P("expert", "dp", None),
        ),
        out_specs=(
            P(("dp", "expert"), None),
            P(("dp", "expert"), None),
            P(("dp", "expert"), None),
            P("expert", None, "dp"),
            P("expert", None, "dp"),
            P("expert", "dp", None),
        ),
        check_vma=False,
    )
```

profile of v0, /device:TPU:0, one launch (start us, length us, event | category | flops | bytes accessed | tf_op | source)
XLA Modules:
  0.0 435.6 jit_solution(945280252774466416)
XLA Ops:
  10.0 2.3 reduce-window.6
  12.9 4.3 scatter_custom_fusion
  17.2 1.2 concatenate.16
  18.5 1.4 gather_fusion.1
  20.1 29.9 %all_to_all.72 = bf16[8,12,3584]{2,1,0:T(8,128)(2,1)S(1)} all-to-all(bf16[8,12,3584]{2,1,0:T(8,128)(2,1)S(1)} %get-tuple-element.37), channel_id=1, replica_groups=mesh['dp'=4,'expert'=8] {'expert'}, dimensions={0} | all-to-all | bytes 1376256 | tf_op jit(solution)/shard_map/all_to_all | solution.py:30
  51.1 26.3 %all_to_all.73 = bf16[8,12,3584]{2,1,0:T(8,128)(2,1)S(1)} all-to-all(bf16[8,12,3584]{2,1,0:T(8,128)(2,1)S(1)} %get-tuple-element.36), channel_id=1, replica_groups=mesh['dp'=4,'expert'=8] {'expert'}, dimensions={0} | all-to-all | bytes 1376256 | tf_op jit(solution)/shard_map/all_to_all | solution.py:30
  78.8 1.4 gather_fusion
  80.4 1.4 gather_fusion.2
  82.9 26.2 %all_to_all.74 = bf16[8,12,3584]{2,1,0:T(8,128)(2,1)S(1)} all-to-all(bf16[8,12,3584]{2,1,0:T(8,128)(2,1)S(1)} %get-tuple-element.34), channel_id=1, replica_groups=mesh['dp'=4,'expert'=8] {'expert'}, dimensions={0} | all-to-all | bytes 1376256 | tf_op jit(solution)/shard_map/all_to_all | solution.py:30
  110.1 26.2 %all_to_all.75 = bf16[8,12,3584]{2,1,0:T(8,128)(2,1)S(1)} all-to-all(bf16[8,12,3584]{2,1,0:T(8,128)(2,1)S(1)} %get-tuple-element.35), channel_id=1, replica_groups=mesh['dp'=4,'expert'=8] {'expert'}, dimensions={0} | all-to-all | bytes 1376256 | tf_op jit(solution)/shard_map/all_to_all | solution.py:30
  137.4 4.6 %fusion.21 = f32[384,512]{1,0:T(8,128)S(1)} fusion(bf16[384,3584]{1,0:T(8,128)(2,1)} %all-gather.7.cloned.1.call-done, bf16[1,3584,512]{2,1,0:T(8,128)(2,1)} %param.11), kind=kOutput, calls=%fused_computation.35 | convolution fusion | flops 1409286144 | bytes 7208960 | tf_op jit(solution)/shard_map/dot_general | solution.py:40
  142.2 2.5 multiply_convert_fusion.5
  145.4 3.1 convolution_convert_fusion
  148.9 4.6 %fusion.23 = f32[384,512]{1,0:T(8,128)S(1)} fusion(bf16[384,3584]{1,0:T(8,128)(2,1)} %all-gather.5.cloned.1.call-done, bf16[1,3584,512]{2,1,0:T(8,128)(2,1)} %param.11), kind=kOutput, calls=%fused_computation.37 | convolution fusion | flops 1409286144 | bytes 7208960 | tf_op jit(solution)/shard_map/dot_general | solution.py:40
  153.6 2.5 multiply_convert_fusion.6
  156.8 3.1 convolution_convert_fusion.1
  160.1 16.6 %all-gather.9.cloned.1.call-done = bf16[384,3584]{1,0:T(8,128)(2,1)} async-done(((bf16[96,3584]{1,0:T(8,128)(2,1)}), bf16[384,3584]{1,0:T(8,128)(2,1)}) %all-gather.9.cloned.1.call-update) | async-done | bytes 2752528 | tf_op jit(solution)/shard_map/all_gather | solution.py:31
  176.7 5.2 %multiply_convert_fusion.3 = (bf16[384,512]{1,0:T(8,128)(2,1)S(1)}, bf16[384,512]{1,0:T(8,128)(2,1)S(1)}) fusion(f32[384,512]{1,0:T(8,128)} %copy-done.24, f32[384,512]{1,0:T(8,128)} %get-tuple-element.16, bf16[384,3584]{1,0:T(8,128)(2,1)} %all-gather.9.cloned.1.call-done, bf16[1,512,3584]{2,1,0:T(8,128)(2,1)} %param.13), kind=kOutput, calls=%fused_computation.46 | convolution fusion | flops 1411842048 | bytes 8781824 | tf_op jit(solution)/shard_map/dot_general | solution.py:18
  181.9 1.6 fusion.19
  183.9 3.2 fusion
  187.2 32.0 %all-gather.11.cloned.1.call-done = bf16[384,3584]{1,0:T(8,128)(2,1)} async-done(((bf16[96,3584]{1,0:T(8,128)(2,1)}), bf16[384,3584]{1,0:T(8,128)(2,1)}) %all-gather.11.cloned.1.call-update) | async-done | bytes 2752528 | tf_op jit(solution)/shard_map/all_gather | solution.py:31
  219.1 5.2 %multiply_convert_fusion.1 = (bf16[384,512]{1,0:T(8,128)(2,1)S(1)}, bf16[384,512]{1,0:T(8,128)(2,1)S(1)}) fusion(f32[384,512]{1,0:T(8,128)} %copy-done.23, f32[384,512]{1,0:T(8,128)} %get-tuple-element.18, bf16[384,3584]{1,0:T(8,128)(2,1)} %all-gather.11.cloned.1.call-done, bf16[1,512,3584]{2,1,0:T(8,128)(2,1)} %param.13), kind=kOutput, calls=%fused_computation.43 | convolution fusion | flops 1411842048 | bytes 8781824 | tf_op jit(solution)/shard_map/dot_general | solution.py:18
  224.4 1.6 fusion.17
  226.7 3.2 fusion.1
  229.9 33.3 %reduce-scatter.7.cloned.1.call-done = bf16[96,3584]{1,0:T(8,128)(2,1)} async-done(((bf16[384,3584]{1,0:T(8,128)(2,1)}), bf16[96,3584]{1,0:T(8,128)(2,1)}) %reduce-scatter.7.cloned.1.call-update) | async-done | bytes 688144 | tf_op jit(solution)/shard_map/reduce_scatter | solution.py:35
  263.3 2.1 all_to_all.54
  265.4 4.6 %all-to-all-start.3 = ((bf16[8,12,3584]{2,1,0:T(8,128)(2,1)}), bf16[8,12,3584]{2,1,0:T(8,128)(2,1)}, u32[]{:S(2)}, u32[]{:S(2)}) async-start(bf16[8,12,3584]{2,1,0:T(8,128)(2,1)} %all_to_all.54), calls=%async_computation.5 | async-start | bytes 1835008 | tf_op jit(solution)/shard_map/all_to_all | solution.py:36
  270.0 37.5 %reduce-scatter.5.cloned.1.call-done = bf16[96,3584]{1,0:T(8,128)(2,1)} async-done(((bf16[384,3584]{1,0:T(8,128)(2,1)}), bf16[96,3584]{1,0:T(8,128)(2,1)}) %reduce-scatter.5.cloned.1.call-update) | async-done | bytes 688144 | tf_op jit(solution)/shard_map/reduce_scatter | solution.py:35
  307.4 2.1 all_to_all.50
  309.5 4.6 %all-to-all-start.1 = ((bf16[8,12,3584]{2,1,0:T(8,128)(2,1)}), bf16[8,12,3584]{2,1,0:T(8,128)(2,1)}, u32[]{:S(2)}, u32[]{:S(2)}) async-start(bf16[8,12,3584]{2,1,0:T(8,128)(2,1)} %all_to_all.50), calls=%async_computation.2 | async-start | bytes 1835008 | tf_op jit(solution)/shard_map/all_to_all | solution.py:36
  314.1 3.9 fusion.42
  318.1 4.1 fusion.3
  322.1 29.6 %reduce-scatter.9.cloned.1.call-done = bf16[96,3584]{1,0:T(8,128)(2,1)} async-done(((bf16[384,3584]{1,0:T(8,128)(2,1)}), bf16[96,3584]{1,0:T(8,128)(2,1)}) %reduce-scatter.9.cloned.1.call-update) | async-done | bytes 688144 | tf_op jit(solution)/shard_map/reduce_scatter | solution.py:35
  351.7 2.1 all_to_all.58
  353.8 4.6 %all-to-all-start.5 = ((bf16[8,12,3584]{2,1,0:T(8,128)(2,1)}), bf16[8,12,3584]{2,1,0:T(8,128)(2,1)}, u32[]{:S(2)}, u32[]{:S(2)}) async-start(bf16[8,12,3584]{2,1,0:T(8,128)(2,1)} %all_to_all.58), calls=%async_computation.8 | async-start | bytes 1835008 | tf_op jit(solution)/shard_map/all_to_all | solution.py:36
  358.4 4.0 fusion.41
  362.5 5.0 %fusion.43 = f32[512,3584]{1,0:T(8,128)} fusion(bf16[384,512]{1,0:T(8,128)(2,1)S(1)} %copy-done.19, bf16[384,3584]{1,0:T(8,128)(2,1)S(1)} %copy-done.10), kind=kOutput, calls=%fused_computation.87 | convolution fusion | flops 1409286144 | bytes 10485760 | tf_op jit(solution)/shard_map/dot_general | solution.py:24
  367.5 4.1 fusion.2
  371.5 23.9 %reduce-scatter.11.cloned.1.call-done = bf16[96,3584]{1,0:T(8,128)(2,1)} async-done(((bf16[384,3584]{1,0:T(8,128)(2,1)}), bf16[96,3584]{1,0:T(8,128)(2,1)}) %reduce-scatter.11.cloned.1.call-update) | async-done | bytes 688144 | tf_op jit(solution)/shard_map/reduce_scatter | solution.py:35
  395.4 2.1 all_to_all.62
  397.5 4.6 %all-to-all-start.7 = ((bf16[8,12,3584]{2,1,0:T(8,128)(2,1)}), bf16[8,12,3584]{2,1,0:T(8,128)(2,1)S(1)}, u32[]{:S(2)}, u32[]{:S(2)}) async-start(bf16[8,12,3584]{2,1,0:T(8,128)(2,1)} %all_to_all.62), calls=%async_computation.11 | async-start | bytes 1835008 | tf_op jit(solution)/shard_map/all_to_all | solution.py:36
  402.1 7.9 %fusion.4 = bf16[1,512,3584]{2,1,0:T(8,128)(2,1)} fusion(f32[512,3584]{1,0:T(8,128)} %fusion.43, bf16[384,512]{1,0:T(8,128)(2,1)S(1)} %copy-done.17, bf16[384,3584]{1,0:T(8,128)(2,1)} %all-gather.11.cloned.1.call-done), kind=kOutput, calls=%fused_computation.16 | convolution fusion | flops 1412956160 | bytes 14155776 | tf_op jit(solution)/shard_map/dot_general | solution.py:24
  410.0 1.9 pad_maximum_fusion
  412.3 1.2 scatter_custom_fusion.1
  414.3 1.8 convolution_convert_fusion.3
  416.1 9.8 %all-to-all-done.7 = bf16[8,12,3584]{2,1,0:T(8,128)(2,1)S(1)} async-done(((bf16[8,12,3584]{2,1,0:T(8,128)(2,1)}), bf16[8,12,3584]{2,1,0:T(8,128)(2,1)S(1)}, u32[]{:S(2)}, u32[]{:S(2)}) %all-to-all-start.7) | async-done | bytes 688160 | tf_op jit(solution)/shard_map/all_to_all | solution.py:36
  425.9 1.5 pad_maximum_fusion.1
  427.4 1.3 convolution_convert_fusion.2
  (106 shorter events, 13.9 us)
Async XLA Ops:
  7.2 130.3 %all-gather.7.cloned.1.call-start = ((), (), s32[]{:S(2)}) async-start(), calls=%async_computation.14 | async-start | bytes 3440640 | tf_op jit(solution)/shard_map/all_gather | solution.py:31
  51.0 27.5 %copy-start.20 = (f32[128,8]{0,1:T(8,128)S(1)}, f32[128,8]{0,1:T(8,128)}, u32[]{:S(2)}) copy-start(f32[128,8]{0,1:T(8,128)} %param.8) | copy-start | bytes 12292
  51.1 29.2 %copy-start.15 = (bf16[128,3584]{1,0:T(8,128)(2,1)S(1)}, bf16[128,3584]{1,0:T(8,128)(2,1)}, u32[]{:S(2)}) copy-start(bf16[128,3584]{1,0:T(8,128)(2,1)} %param.10) | copy-start | bytes 2752516
  51.1 97.8 %all-gather.5.cloned.1.call-start = ((), (), s32[]{:S(2)}) async-start(), calls=%async_computation.12 | async-start | bytes 3440640 | tf_op jit(solution)/shard_map/all_gather | solution.py:31
  78.5 98.2 %all-gather.9.cloned.1.call-start = ((), (), s32[]{:S(2)}) async-start(), calls=%async_computation.16 | async-start | bytes 3440640 | tf_op jit(solution)/shard_map/all_gather | solution.py:31
  81.8 1.1 copy-start.8
  110.1 109.0 %all-gather.11.cloned.1.call-start = ((), (), s32[]{:S(2)}) async-start(), calls=%async_computation.18 | async-start | bytes 3440640 | tf_op jit(solution)/shard_map/all_gather | solution.py:31
  137.4 125.9 %reduce-scatter.7.cloned.1.call-start = ((), (), s32[]{:S(2)}) async-start(), calls=%async_computation.15 | async-start | bytes 3440640 | tf_op jit(solution)/shard_map/reduce_scatter | solution.py:35
  137.4 4.6 %copy-start = (bf16[384,3584]{1,0:T(8,128)(2,1)S(1)}, bf16[384,3584]{1,0:T(8,128)(2,1)}, u32[]{:S(2)}) copy-start(bf16[384,3584]{1,0:T(8,128)(2,1)} %all-gather.7.cloned.1.call-done) | copy-start | bytes 8257540
  137.4 4.8 %copy-start.3 = (bf16[1,3584,512]{2,1,0:T(8,128)(2,1)S(1)}, bf16[1,3584,512]{2,1,0:T(8,128)(2,1)}, u32[]{:S(2)}) copy-start(bf16[1,3584,512]{2,1,0:T(8,128)(2,1)} %param.12) | copy-start | bytes 11010052
  142.2 2.5 copy-start.23
  142.2 3.2 copy-start.21
  144.7 0.8 copy-start.16
  148.6 158.8 %reduce-scatter.5.cloned.1.call-start = ((), (), s32[]{:S(2)}) async-start(), calls=%async_computation.13 | async-start | bytes 3440640 | tf_op jit(solution)/shard_map/reduce_scatter | solution.py:35
  148.8 4.6 %copy-start.4 = (bf16[1,3584,512]{2,1,0:T(8,128)(2,1)S(1)}, bf16[1,3584,512]{2,1,0:T(8,128)(2,1)}, u32[]{:S(2)}) copy-start(bf16[1,3584,512]{2,1,0:T(8,128)(2,1)} %param.12) | copy-start | bytes 11010052
  148.9 4.8 %copy-start.7 = (bf16[384,3584]{1,0:T(8,128)(2,1)S(1)}, bf16[384,3584]{1,0:T(8,128)(2,1)}, u32[]{:S(2)}) copy-start(bf16[384,3584]{1,0:T(8,128)(2,1)} %all-gather.5.cloned.1.call-done) | copy-start | bytes 8257540
  153.6 2.5 copy-start.24
  153.6 3.2 copy-start.22
  156.1 0.7 copy-start.18
  160.0 191.7 %reduce-scatter.9.cloned.1.call-start = ((), (), s32[]{:S(2)}) async-start(), calls=%async_computation.17 | async-start | bytes 3440640 | tf_op jit(solution)/shard_map/reduce_scatter | solution.py:35
  176.7 5.2 %copy-start.1 = (bf16[1,3584,512]{2,1,0:T(8,128)(2,1)S(1)}, bf16[1,3584,512]{2,1,0:T(8,128)(2,1)}, u32[]{:S(2)}) copy-start(bf16[1,3584,512]{2,1,0:T(8,128)(2,1)} %param.11) | copy-start | bytes 11010052
  181.9 2.0 copy-start.5
  187.1 208.3 %reduce-scatter.11.cloned.1.call-start = ((), (), s32[]{:S(2)}) async-start(), calls=%async_computation.19 | async-start | bytes 3440640 | tf_op jit(solution)/shard_map/reduce_scatter | solution.py:35
  219.1 5.2 %copy-start.2 = (bf16[1,3584,512]{2,1,0:T(8,128)(2,1)S(1)}, bf16[1,3584,512]{2,1,0:T(8,128)(2,1)}, u32[]{:S(2)}) copy-start(bf16[1,3584,512]{2,1,0:T(8,128)(2,1)} %param.11) | copy-start | bytes 11010052
  224.3 1.7 copy-start.11
  224.3 1.7 copy-start.13
  224.4 2.3 copy-start.6
  265.4 44.1 %all-to-all-start.3 = ((bf16[8,12,3584]{2,1,0:T(8,128)(2,1)}), bf16[8,12,3584]{2,1,0:T(8,128)(2,1)}, u32[]{:S(2)}, u32[]{:S(2)}) async-start(bf16[8,12,3584]{2,1,0:T(8,128)(2,1)} %all_to_all.54), calls=%async_computation.5 | async-start | bytes 1835008 | tf_op jit(solution)/shard_map/all_to_all | solution.py:36
  309.5 44.3 %all-to-all-start.1 = ((bf16[8,12,3584]{2,1,0:T(8,128)(2,1)}), bf16[8,12,3584]{2,1,0:T(8,128)(2,1)}, u32[]{:S(2)}, u32[]{:S(2)}) async-start(bf16[8,12,3584]{2,1,0:T(8,128)(2,1)} %all_to_all.50), calls=%async_computation.2 | async-start | bytes 1835008 | tf_op jit(solution)/shard_map/all_to_all | solution.py:36
  314.1 3.9 copy-start.14
  353.8 43.7 %all-to-all-start.5 = ((bf16[8,12,3584]{2,1,0:T(8,128)(2,1)}), bf16[8,12,3584]{2,1,0:T(8,128)(2,1)}, u32[]{:S(2)}, u32[]{:S(2)}) async-start(bf16[8,12,3584]{2,1,0:T(8,128)(2,1)} %all_to_all.58), calls=%async_computation.8 | async-start | bytes 1835008 | tf_op jit(solution)/shard_map/all_to_all | solution.py:36
  358.4 4.0 copy-start.10
  358.4 4.1 copy-start.19
  362.4 5.0 %copy-start.12 = (bf16[384,512]{1,0:T(8,128)(2,1)S(1)}, bf16[384,512]{1,0:T(8,128)(2,1)}, u32[]{:S(2)}) copy-start(bf16[384,512]{1,0:T(8,128)(2,1)} %copy-done.11) | copy-start | bytes 1179652
  371.5 30.5 %copy-start.17 = (bf16[384,512]{1,0:T(8,128)(2,1)S(1)}, bf16[384,512]{1,0:T(8,128)(2,1)}, u32[]{:S(2)}) copy-start(bf16[384,512]{1,0:T(8,128)(2,1)} %copy-done.16) | copy-start | bytes 1179652
  397.5 28.4 %all-to-all-start.7 = ((bf16[8,12,3584]{2,1,0:T(8,128)(2,1)}), bf16[8,12,3584]{2,1,0:T(8,128)(2,1)S(1)}, u32[]{:S(2)}, u32[]{:S(2)}) async-start(bf16[8,12,3584]{2,1,0:T(8,128)(2,1)} %all_to_all.62), calls=%async_computation.11 | async-start | bytes 1835008 | tf_op jit(solution)/shard_map/all_to_all | solution.py:36
  410.0 1.9 copy-start.9
Sparse Core Ops, SparseCore 0:
  51.2 39.6 all-gather.6
  93.3 40.7 all-gather.4
  135.9 40.7 all-gather.8
  178.4 40.7 all-gather.10
  222.6 40.6 reduce-scatter.6
  266.7 40.6 reduce-scatter.4
  311.0 40.6 reduce-scatter.8
  354.7 40.6 reduce-scatter.10
where the time goes:
time: 436 us
  waiting for transfers between devices  183 us (42%)
  blocking collectives  109 us (25%)
  matrix products  72.5 us (17%)
  local copies, waits for them, and re-layouts  30.1 us (7%)
  starting transfers between devices  18.9 us (4%)
  between operations  14.6 us (3%)
  other arithmetic  8.13 us (2%)
    reduce_scatter x4, waiting for transfers between devices, gather_back(): lax.psum_scatter(partial_rows, 'dp', scatter_dimension=0, tiled=True)  124 us
    all_to_all x4, blocking collectives, dispatch(): lax.all_to_all(send_rows, 'expert', split_axis=0, concat_axis=0, tiled=True)  109 us
    all_gather x4, waiting for transfers between devices, dispatch(): return lax.all_gather(along_expert, 'dp', axis=0, tiled=True)  48.6 us
    dot_general x6, matrix products, contract_first(): lax.dot_general(left, right, (((0,), (0,)), ((), ())), preferred_element_...  29 us
    dot_general x6, matrix products, contract_last(): lax.dot_general(left, right, (((1,), (1,)), ((), ())), preferred_element_...  20 us
    all_to_all x4, starting transfers between devices, gather_back(): lax.all_to_all(summed, 'expert', split_axis=0, concat_axis=0, tiled=True)  18.4 us
    all_to_all x4, waiting for transfers between devices, gather_back(): lax.all_to_all(summed, 'expert', split_axis=0, concat_axis=0, tiled=True)  9.8 us
    dot_general x2, matrix products, expert_forward(): gate_pre = jnp.dot(rows_x, gate_w, preferred_element_type=jnp.float32)  9.19 us
  transfers between devices with their start and end apart: 12, of which 7 were waited for; matrix products, arithmetic and copies ran while one was open for 18% of the time, Pallas kernels for 0%

commit v1 on v0

--- a/solution.py
+++ b/solution.py
@@ -2,6 +2,19 @@
 import jax.numpy as jnp
 from jax import lax
 from jax.sharding import PartitionSpec as P
+
+
+def ring_gather(array, axis, dim):
+    ways = lax.axis_size(axis)
+    up = [(d, (d + 1) % ways) for d in range(ways)]
+    down = [(d, (d - 1) % ways) for d in range(ways)]
+    earlier, later = ([array], [array])
+    for _ in range(ways // 2):
+        earlier.append(lax.ppermute(earlier[-1], axis, up))
+    for _ in range((ways - 1) // 2):
+        later.append(lax.ppermute(later[-1], axis, down))
+    line = jnp.concatenate([*earlier[::-1], *later[1:]], axis=dim)
+    return jnp.roll(line, (lax.axis_index(axis) - ways // 2) * array.shape[dim], axis=dim)
 
 
 def slot_table(flat_ids, experts, capacity, sentinel):
@@ -28,7 +41,7 @@
 
 def dispatch(send_rows):
     along_expert = lax.all_to_all(send_rows, "expert", split_axis=0, concat_axis=0, tiled=True)
-    return lax.all_gather(along_expert, "dp", axis=0, tiled=True)
+    return ring_gather(along_expert, "dp", 0)
 
 
 def gather_back(partial_rows, groups):

time: 436 us -> 553 us (1.27)
  waiting for transfers between devices: 183 us -> 247 us
  other arithmetic: 8.13 us -> 54.4 us
  matrix products: 72.5 us -> 59 us
  starting transfers between devices: 18.9 us -> 30.3 us
    ppermute x0 -> x12, waiting for transfers between devices: none -> 193 us  [the longest x8 139 us: ring_gather(): earlier.append(lax.ppermute(earlier[-1], axis, up))]
    reduce_scatter x4, waiting for transfers between devices: 124 us -> 0.04 us  [gather_back(): lax.psum_scatter(partial_rows, 'dp', scatter_dimension=0, tiled=True)]
    all_gather x4 -> x0, waiting for transfers between devices: 48.6 us -> none  [dispatch(): return lax.all_gather(along_expert, 'dp', axis=0, tiled=True)]
    concatenate x0 -> x4, other arithmetic: none -> 45.1 us  [ring_gather(): jnp.roll(line, (lax.axis_index(axis) - ways // 2) * array.shape[dim], axi...]
    all_to_all x4, waiting for transfers between devices: 9.8 us -> 54.2 us  [gather_back(): lax.all_to_all(summed, 'expert', split_axis=0, concat_axis=0, tiled=True)]
    ppermute x0 -> x12, starting transfers between devices: none -> 13.4 us  [the longest x4 9.66 us: ring_gather(): later.append(lax.ppermute(later[-1], axis, down))]
    dot_general x6, matrix products: 20 us -> 13.1 us  [contract_last(): lax.dot_general(left, right, (((1,), (1,)), ((), ())), preferred_element_...]
    dot_general x2, matrix products: 9.19 us -> 3.15 us  [expert_forward(): gate_pre = jnp.dot(rows_x, gate_w, preferred_element_type=jnp.float32)]
  transfers between devices with their start and end apart: 12 -> 20, of which waited for: 7 -> 16; matrix products, arithmetic and copies ran while one was open for 18% -> 17% of each run, Pallas kernels for 0% -> 0%
where the time goes in v1:
time: 553 us; the launch traced here: 548 us
  waiting for transfers between devices  247 us (45%)
  blocking collectives  110 us (20%)
  matrix products  59 us (11%)
  other arithmetic  54.4 us (10%)
  local copies, waits for them, and re-layouts  33.5 us (6%)
  starting transfers between devices  30.3 us (5%)
  between operations  14.8 us (3%)
    ppermute x8, waiting for transfers between devices, ring_gather(): earlier.append(lax.ppermute(earlier[-1], axis, up))  139 us
    all_to_all x4, blocking collectives, dispatch(): lax.all_to_all(send_rows, 'expert', split_axis=0, concat_axis=0, tiled=True)  110 us
    all_to_all x4, waiting for transfers between devices, gather_back(): lax.all_to_all(summed, 'expert', split_axis=0, concat_axis=0, tiled=True)  54.2 us
    ppermute x4, waiting for transfers between devices, ring_gather(): later.append(lax.ppermute(later[-1], axis, down))  53.8 us
    concatenate x4, other arithmetic, ring_gather(): jnp.roll(line, (lax.axis_index(axis) - ways // 2) * array.shape[dim], axi...  45.1 us
    dot_general x6, matrix products, contract_first(): lax.dot_general(left, right, (((0,), (0,)), ((), ())), preferred_element_...  28.3 us
    all_to_all x4, starting transfers between devices, gather_back(): lax.all_to_all(summed, 'expert', split_axis=0, concat_axis=0, tiled=True)  16.7 us
    dot_general x6, matrix products, contract_last(): lax.dot_general(left, right, (((1,), (1,)), ((), ())), preferred_element_...  13.1 us
  transfers between devices with their start and end apart: 20, of which 16 were waited for; matrix products, arithmetic and copies ran while one was open for 17% of the time, Pallas kernels for 0%

profile of v1, /device:TPU:0, one launch (start us, length us, event | category | flops | bytes accessed | tf_op | source)
XLA Modules:
  0.0 548.4 jit_solution(10679241483964552094)
XLA Ops:
  10.0 2.3 reduce-window.6
  12.9 4.3 scatter_custom_fusion
  20.1 29.9 %all_to_all.72 = bf16[8,12,3584]{2,1,0:T(8,128)(2,1)S(1)} all-to-all(bf16[8,12,3584]{2,1,0:T(8,128)(2,1)S(1)} %get-tuple-element.37), channel_id=1, replica_groups=mesh['dp'=4,'expert'=8] {'expert'}, dimensions={0} | all-to-all | bytes 1376256 | tf_op jit(solution)/shard_map/all_to_all | solution.py:43
  53.2 16.3 %collective-permute-done = bf16[96,3584]{1,0:T(8,128)(2,1)S(1)} collective-permute-done((bf16[96,3584]{1,0:T(8,128)(2,1)S(1)}, bf16[96,3584]{1,0:T(8,128)(2,1)S(1)}, u32[]{:S(2)}, u32[]{:S(2)}) %collective-permute-start) | collective-permute-done | bytes 688160 | tf_op jit(solution)/shard_map/ppermute | solution.py:13
  70.2 14.1 %collective-permute-done.2 = bf16[96,3584]{1,0:T(8,128)(2,1)S(1)} collective-permute-done((bf16[96,3584]{1,0:T(8,128)(2,1)S(1)}, bf16[96,3584]{1,0:T(8,128)(2,1)S(1)}, u32[]{:S(2)}, u32[]{:S(2)}) %collective-permute-start.2) | collective-permute-done | bytes 688160 | tf_op jit(solution)/shard_map/ppermute | solution.py:15
  84.3 13.4 %collective-permute-done.1 = bf16[96,3584]{1,0:T(8,128)(2,1)} collective-permute-done((bf16[96,3584]{1,0:T(8,128)(2,1)S(1)}, bf16[96,3584]{1,0:T(8,128)(2,1)}, u32[]{:S(2)}, u32[]{:S(2)}) %collective-permute-start.1) | collective-permute-done | bytes 688160 | tf_op jit(solution)/shard_map/ppermute | solution.py:13
  97.7 11.4 %fusion.49 = bf16[384,3584]{1,0:T(8,128)(2,1)S(1)} fusion(s32[]{:T(128)S(6)} %select_n.56, bf16[96,3584]{1,0:T(8,128)(2,1)} %collective-permute-done.1, bf16[96,3584]{1,0:T(8,128)(2,1)S(1)} %collective-permute-done, bf16[96,3584]{1,0:T(8,128)(2,1)S(1)} %all_to_all.49, bf16[96,3584]{1,0:T(8,128)(2,1)S(1)} %collective-permute-done.2), kind=kLoop, calls=%fused_computation.95 | loop fusion | flops 22020096 | bytes 5505028 | tf_op jit(solution)/shard_map/jit(_roll_dynamic)/concatenate | solution.py:17
  112.2 2.5 multiply_convert_fusion.6
  115.4 3.1 convolution_convert_fusion.1
  118.6 26.6 %all_to_all.73 = bf16[8,12,3584]{2,1,0:T(8,128)(2,1)S(1)} all-to-all(bf16[8,12,3584]{2,1,0:T(8,128)(2,1)S(1)} %get-tuple-element.38), channel_id=1, replica_groups=mesh['dp'=4,'expert'=8] {'expert'}, dimensions={0} | all-to-all | bytes 1376256 | tf_op jit(solution)/shard_map/all_to_all | solution.py:43
  150.4 2.4 collective-permute-start.5
  152.8 19.3 %collective-permute-done.3 = bf16[96,3584]{1,0:T(8,128)(2,1)} collective-permute-done((bf16[96,3584]{1,0:T(8,128)(2,1)S(1)}, bf16[96,3584]{1,0:T(8,128)(2,1)}, u32[]{:S(2)}, u32[]{:S(2)}) %collective-permute-start.3) | collective-permute-done | bytes 688160 | tf_op jit(solution)/shard_map/ppermute | solution.py:13
  173.7 12.3 %collective-permute-done.5 = bf16[96,3584]{1,0:T(8,128)(2,1)S(1)} collective-permute-done((bf16[96,3584]{1,0:T(8,128)(2,1)S(1)}, bf16[96,3584]{1,0:T(8,128)(2,1)S(1)}, u32[]{:S(2)}, u32[]{:S(2)}) %collective-permute-start.5) | collective-permute-done | bytes 688160 | tf_op jit(solution)/shard_map/ppermute | solution.py:15
  186.1 14.1 %collective-permute-done.4 = bf16[96,3584]{1,0:T(8,128)(2,1)S(1)} collective-permute-done((bf16[96,3584]{1,0:T(8,128)(2,1)}, bf16[96,3584]{1,0:T(8,128)(2,1)S(1)}, u32[]{:S(2)}, u32[]{:S(2)}) %collective-permute-start.4) | collective-permute-done | bytes 688160 | tf_op jit(solution)/shard_map/ppermute | solution.py:13
  200.1 11.2 %fusion.42 = bf16[384,3584]{1,0:T(8,128)(2,1)S(1)} fusion(s32[]{:T(128)S(6)} %select_n.56, bf16[96,3584]{1,0:T(8,128)(2,1)S(1)} %collective-permute-done.4, bf16[96,3584]{1,0:T(8,128)(2,1)} %collective-permute-done.3, bf16[96,3584]{1,0:T(8,128)(2,1)S(1)} %all_to_all.53, bf16[96,3584]{1,0:T(8,128)(2,1)S(1)} %collective-permute-done.5), kind=kLoop, calls=%fused_computation.88 | loop fusion | flops 22020096 | bytes 5505028 | tf_op jit(solution)/shard_map/jit(_roll_dynamic)/concatenate | solution.py:17
  214.4 2.5 multiply_convert_fusion.5
  217.7 3.1 convolution_convert_fusion
  221.1 26.5 %all_to_all.74 = bf16[8,12,3584]{2,1,0:T(8,128)(2,1)S(1)} all-to-all(bf16[8,12,3584]{2,1,0:T(8,128)(2,1)S(1)} %get-tuple-element.36), channel_id=1, replica_groups=mesh['dp'=4,'expert'=8] {'expert'}, dimensions={0} | all-to-all | bytes 1376256 | tf_op jit(solution)/shard_map/all_to_all | solution.py:43
  247.9 2.9 collective-permute-start.11
  250.8 23.6 %collective-permute-done.9 = bf16[96,3584]{1,0:T(8,128)(2,1)S(1)} collective-permute-done((bf16[96,3584]{1,0:T(8,128)(2,1)S(1)}, bf16[96,3584]{1,0:T(8,128)(2,1)S(1)}, u32[]{:S(2)}, u32[]{:S(2)}) %collective-permute-start.9) | collective-permute-done | bytes 688160 | tf_op jit(solution)/shard_map/ppermute | solution.py:13
  274.8 13.6 %collective-permute-done.11 = bf16[96,3584]{1,0:T(8,128)(2,1)S(1)} collective-permute-done((bf16[96,3584]{1,0:T(8,128)(2,1)S(1)}, bf16[96,3584]{1,0:T(8,128)(2,1)S(1)}, u32[]{:S(2)}, u32[]{:S(2)}) %collective-permute-start.11) | collective-permute-done | bytes 688160 | tf_op jit(solution)/shard_map/ppermute | solution.py:15
  288.4 14.2 %collective-permute-done.10 = bf16[96,3584]{1,0:T(8,128)(2,1)S(1)} collective-permute-done((bf16[96,3584]{1,0:T(8,128)(2,1)S(1)}, bf16[96,3584]{1,0:T(8,128)(2,1)S(1)}, u32[]{:S(2)}, u32[]{:S(2)}) %collective-permute-start.10) | collective-permute-done | bytes 688160 | tf_op jit(solution)/shard_map/ppermute | solution.py:13
  302.6 11.3 %fusion.28 = bf16[384,3584]{1,0:T(8,128)(2,1)S(1)} fusion(s32[]{:T(128)S(6)} %select_n.56, bf16[96,3584]{1,0:T(8,128)(2,1)S(1)} %collective-permute-done.10, bf16[96,3584]{1,0:T(8,128)(2,1)S(1)} %collective-permute-done.9, bf16[96,3584]{1,0:T(8,128)(2,1)S(1)} %all_to_all.61, bf16[96,3584]{1,0:T(8,128)(2,1)S(1)} %collective-permute-done.11), kind=kLoop, calls=%fused_computation.74 | loop fusion | flops 22020096 | bytes 5505028 | tf_op jit(solution)/shard_map/jit(_roll_dynamic)/concatenate | solution.py:17
  319.0 3.2 fusion.1
  322.3 26.6 %all_to_all.75 = bf16[8,12,3584]{2,1,0:T(8,128)(2,1)S(1)} all-to-all(bf16[8,12,3584]{2,1,0:T(8,128)(2,1)S(1)} %get-tuple-element.35), channel_id=1, replica_groups=mesh['dp'=4,'expert'=8] {'expert'}, dimensions={0} | all-to-all | bytes 1376256 | tf_op jit(solution)/shard_map/all_to_all | solution.py:43
  349.1 2.9 collective-permute-start.8
  352.0 23.7 %collective-permute-done.6 = bf16[96,3584]{1,0:T(8,128)(2,1)S(1)} collective-permute-done((bf16[96,3584]{1,0:T(8,128)(2,1)S(1)}, bf16[96,3584]{1,0:T(8,128)(2,1)S(1)}, u32[]{:S(2)}, u32[]{:S(2)}) %collective-permute-start.6) | collective-permute-done | bytes 688160 | tf_op jit(solution)/shard_map/ppermute | solution.py:13
  375.9 13.8 %collective-permute-done.8 = bf16[96,3584]{1,0:T(8,128)(2,1)S(1)} collective-permute-done((bf16[96,3584]{1,0:T(8,128)(2,1)S(1)}, bf16[96,3584]{1,0:T(8,128)(2,1)S(1)}, u32[]{:S(2)}, u32[]{:S(2)}) %collective-permute-start.8) | collective-permute-done | bytes 688160 | tf_op jit(solution)/shard_map/ppermute | solution.py:15
  389.7 14.2 %collective-permute-done.7 = bf16[96,3584]{1,0:T(8,128)(2,1)S(1)} collective-permute-done((bf16[96,3584]{1,0:T(8,128)(2,1)S(1)}, bf16[96,3584]{1,0:T(8,128)(2,1)S(1)}, u32[]{:S(2)}, u32[]{:S(2)}) %collective-permute-start.7) | collective-permute-done | bytes 688160 | tf_op jit(solution)/shard_map/ppermute | solution.py:13
  403.8 11.3 %fusion.35 = bf16[384,3584]{1,0:T(8,128)(2,1)S(1)} fusion(s32[]{:T(128)S(6)} %select_n.56, bf16[96,3584]{1,0:T(8,128)(2,1)S(1)} %collective-permute-done.7, bf16[96,3584]{1,0:T(8,128)(2,1)S(1)} %collective-permute-done.6, bf16[96,3584]{1,0:T(8,128)(2,1)S(1)} %all_to_all.57, bf16[96,3584]{1,0:T(8,128)(2,1)S(1)} %collective-permute-done.8), kind=kLoop, calls=%fused_computation.81 | loop fusion | flops 22020096 | bytes 5505028 | tf_op jit(solution)/shard_map/jit(_roll_dynamic)/concatenate | solution.py:17
  420.5 3.1 fusion
  423.7 2.1 all_to_all.50
  425.8 3.6 all-to-all-start.1
  429.4 2.1 all_to_all.54
  431.5 21.6 %all-to-all-done.1 = bf16[8,12,3584]{2,1,0:T(8,128)(2,1)S(1)} async-done(((bf16[8,12,3584]{2,1,0:T(8,128)(2,1)}), bf16[8,12,3584]{2,1,0:T(8,128)(2,1)S(1)}, u32[]{:S(2)}, u32[]{:S(2)}) %all-to-all-start.1) | async-done | bytes 688160 | tf_op jit(solution)/shard_map/all_to_all | solution.py:49
  454.0 4.4 all-to-all-start.3
  458.4 4.1 fusion.70
  462.5 4.1 fusion.3
  468.7 13.5 %all-to-all-done.3 = bf16[8,12,3584]{2,1,0:T(8,128)(2,1)} async-done(((bf16[8,12,3584]{2,1,0:T(8,128)(2,1)}), bf16[8,12,3584]{2,1,0:T(8,128)(2,1)}, u32[]{:S(2)}, u32[]{:S(2)}) %all-to-all-start.3) | async-done | bytes 688160 | tf_op jit(solution)/shard_map/all_to_all | solution.py:49
  482.2 4.2 all-to-all-start.7
  486.5 4.0 fusion.69
  490.5 5.0 fusion.71
  495.5 4.1 fusion.2
  499.6 2.2 all_to_all.58
  501.8 8.4 %all-to-all-done.7 = bf16[8,12,3584]{2,1,0:T(8,128)(2,1)} async-done(((bf16[8,12,3584]{2,1,0:T(8,128)(2,1)}), bf16[8,12,3584]{2,1,0:T(8,128)(2,1)}, u32[]{:S(2)}, u32[]{:S(2)}) %all-to-all-start.7) | async-done | bytes 688160 | tf_op jit(solution)/shard_map/all_to_all | solution.py:49
  510.2 4.5 all-to-all-start.5
  514.8 7.1 %fusion.4 = bf16[1,512,3584]{2,1,0:T(8,128)(2,1)} fusion(f32[512,3584]{1,0:T(8,128)} %fusion.71, bf16[384,512]{1,0:T(8,128)(2,1)S(1)} %copy-done.25, bf16[384,3584]{1,0:T(8,128)(2,1)S(1)} %copy-done.16), kind=kOutput, calls=%fused_computation.48 | convolution fusion | flops 1412956160 | bytes 14155776 | tf_op jit(solution)/shard_map/dot_general | solution.py:37
  527.8 10.7 %all-to-all-done.5 = bf16[8,12,3584]{2,1,0:T(8,128)(2,1)} async-done(((bf16[8,12,3584]{2,1,0:T(8,128)(2,1)}), bf16[8,12,3584]{2,1,0:T(8,128)(2,1)}, u32[]{:S(2)}, u32[]{:S(2)}) %all-to-all-start.5) | async-done | bytes 688160 | tf_op jit(solution)/shard_map/all_to_all | solution.py:49
  (150 shorter events, 48.4 us)
Async XLA Ops:
  7.2 416.5 %reduce-scatter.5.cloned.1.call-start = ((), (), s32[]{:S(2)}) async-start(), calls=%async_computation.12 | async-start | bytes 3440640 | tf_op jit(solution)/shard_map/reduce_scatter | solution.py:48
  50.2 19.3 %collective-permute-start = (bf16[96,3584]{1,0:T(8,128)(2,1)S(1)}, bf16[96,3584]{1,0:T(8,128)(2,1)S(1)}, u32[]{:S(2)}, u32[]{:S(2)}) collective-permute-start(bf16[96,3584]{1,0:T(8,128)(2,1)S(1)} %all_to_all.49), channel_id=1, source_target_pairs={{0,8},{8,16},{16,24},{24,0},{1,9},{9,17},{17,25},{25,1},{2,10},{10... | collective-permute-start | bytes 2064392 | tf_op jit(solution)/shard_map/ppermute | solution.py:13
  51.7 32.6 %collective-permute-start.2 = (bf16[96,3584]{1,0:T(8,128)(2,1)S(1)}, bf16[96,3584]{1,0:T(8,128)(2,1)S(1)}, u32[]{:S(2)}, u32[]{:S(2)}) collective-permute-start(bf16[96,3584]{1,0:T(8,128)(2,1)S(1)} %all_to_all.49), channel_id=1, source_target_pairs={{0,24},{8,0},{16,8},{24,16},{1,25},{9,1},{17,9},{25,17},{2,26},{10... | collective-permute-start | bytes 2064392 | tf_op jit(solution)/shard_map/ppermute | solution.py:15
  69.5 28.2 %collective-permute-start.1 = (bf16[96,3584]{1,0:T(8,128)(2,1)S(1)}, bf16[96,3584]{1,0:T(8,128)(2,1)}, u32[]{:S(2)}, u32[]{:S(2)}) collective-permute-start(bf16[96,3584]{1,0:T(8,128)(2,1)S(1)} %collective-permute-done), channel_id=1, source_target_pairs={{0,8},{8,16},{16,24},{24,0},{1,9},{9,17},{17,25},{25,1},{2,10},{10... | collective-permute-start | bytes 2064392 | tf_op jit(solution)/shard_map/ppermute | solution.py:13
  70.2 38.9 %copy-start.3 = (bf16[1,3584,512]{2,1,0:T(8,128)(2,1)S(1)}, bf16[1,3584,512]{2,1,0:T(8,128)(2,1)}, u32[]{:S(2)}) copy-start(bf16[1,3584,512]{2,1,0:T(8,128)(2,1)} %param.13) | copy-start | bytes 11010052
  109.1 3.0 copy-start.7
  112.2 2.5 copy-start.33
  112.2 3.2 copy-start.29
  118.6 27.4 %copy-start.28 = (f32[128,8]{0,1:T(8,128)S(1)}, f32[128,8]{0,1:T(8,128)}, u32[]{:S(2)}) copy-start(f32[128,8]{0,1:T(8,128)} %param.10) | copy-start | bytes 12292
  118.6 310.8 %reduce-scatter.7.cloned.1.call-start = ((), (), s32[]{:S(2)}) async-start(), calls=%async_computation.13 | async-start | bytes 3440640 | tf_op jit(solution)/shard_map/reduce_scatter | solution.py:48
  145.3 26.8 %collective-permute-start.3 = (bf16[96,3584]{1,0:T(8,128)(2,1)S(1)}, bf16[96,3584]{1,0:T(8,128)(2,1)}, u32[]{:S(2)}, u32[]{:S(2)}) collective-permute-start(bf16[96,3584]{1,0:T(8,128)(2,1)S(1)} %all_to_all.53), channel_id=1, source_target_pairs={{0,8},{8,16},{16,24},{24,0},{1,9},{9,17},{17,25},{25,1},{2,10},{10... | collective-permute-start | bytes 2064392 | tf_op jit(solution)/shard_map/ppermute | solution.py:13
  150.4 60.9 %copy-start.11 = (bf16[192,3584]{1,0:T(8,128)(2,1)}, bf16[192,3584]{1,0:T(8,128)(2,1)S(1)}, u32[]{:S(2)}) copy-start(bf16[192,3584]{1,0:T(8,128)(2,1)S(1)} %gather_fusion.2) | copy-start | bytes 4128772
  150.4 35.7 %collective-permute-start.5 = (bf16[96,3584]{1,0:T(8,128)(2,1)S(1)}, bf16[96,3584]{1,0:T(8,128)(2,1)S(1)}, u32[]{:S(2)}, u32[]{:S(2)}) collective-permute-start(bf16[96,3584]{1,0:T(8,128)(2,1)S(1)} %all_to_all.53), channel_id=1, source_target_pairs={{0,24},{8,0},{16,8},{24,16},{1,25},{9,1},{17,9},{25,17},{2,26},{10... | collective-permute-start | bytes 2064392 | tf_op jit(solution)/shard_map/ppermute | solution.py:15
  172.1 28.0 %collective-permute-start.4 = (bf16[96,3584]{1,0:T(8,128)(2,1)}, bf16[96,3584]{1,0:T(8,128)(2,1)S(1)}, u32[]{:S(2)}, u32[]{:S(2)}) collective-permute-start(bf16[96,3584]{1,0:T(8,128)(2,1)} %collective-permute-done.3), channel_id=1, source_target_pairs={{0,8},{8,16},{16,24},{24,0},{1,9},{9,17},{17,25},{25,1},{2,10},{10... | collective-permute-start | bytes 2064392 | tf_op jit(solution)/shard_map/ppermute | solution.py:13
  172.3 39.0 %copy-start.4 = (bf16[1,3584,512]{2,1,0:T(8,128)(2,1)S(1)}, bf16[1,3584,512]{2,1,0:T(8,128)(2,1)}, u32[]{:S(2)}) copy-start(bf16[1,3584,512]{2,1,0:T(8,128)(2,1)} %param.13) | copy-start | bytes 11010052
  211.4 3.0 copy-start.8
  214.4 3.2 copy-start.30
  217.6 3.2 copy-start.17
  220.8 245.8 %reduce-scatter.11.cloned.1.call-start = ((), (), s32[]{:S(2)}) async-start(), calls=%async_computation.15 | async-start | bytes 3440640 | tf_op jit(solution)/shard_map/reduce_scatter | solution.py:48
  247.8 66.1 %copy-start.31 = (bf16[1,512,3584]{2,1,0:T(8,128)(2,1)S(1)}, bf16[1,512,3584]{2,1,0:T(8,128)(2,1)}, u32[]{:S(2)}) copy-start(bf16[1,512,3584]{2,1,0:T(8,128)(2,1)} %param.15) | copy-start | bytes 11010052
  247.8 66.1 %copy-start.36 = (f32[384,512]{1,0:T(8,128)S(1)}, f32[384,512]{1,0:T(8,128)}, u32[]{:S(2)}) copy-start(f32[384,512]{1,0:T(8,128)} %copy-done.35) | copy-start | bytes 2359300
  247.8 66.1 %copy-start.38 = (f32[384,512]{1,0:T(8,128)S(1)}, f32[384,512]{1,0:T(8,128)}, u32[]{:S(2)}) copy-start(f32[384,512]{1,0:T(8,128)} %get-tuple-element.19) | copy-start | bytes 2359300
  247.8 26.5 %collective-permute-start.9 = (bf16[96,3584]{1,0:T(8,128)(2,1)S(1)}, bf16[96,3584]{1,0:T(8,128)(2,1)S(1)}, u32[]{:S(2)}, u32[]{:S(2)}) collective-permute-start(bf16[96,3584]{1,0:T(8,128)(2,1)S(1)} %all_to_all.61), channel_id=1, source_target_pairs={{0,8},{8,16},{16,24},{24,0},{1,9},{9,17},{17,25},{25,1},{2,10},{10... | collective-permute-start | bytes 2064392 | tf_op jit(solution)/shard_map/ppermute | solution.py:13
  247.9 40.5 %collective-permute-start.11 = (bf16[96,3584]{1,0:T(8,128)(2,1)S(1)}, bf16[96,3584]{1,0:T(8,128)(2,1)S(1)}, u32[]{:S(2)}, u32[]{:S(2)}) collective-permute-start(bf16[96,3584]{1,0:T(8,128)(2,1)S(1)} %all_to_all.61), channel_id=1, source_target_pairs={{0,24},{8,0},{16,8},{24,16},{1,25},{9,1},{17,9},{25,17},{2,26},{10... | collective-permute-start | bytes 2064392 | tf_op jit(solution)/shard_map/ppermute | solution.py:15
  274.4 28.3 %collective-permute-start.10 = (bf16[96,3584]{1,0:T(8,128)(2,1)S(1)}, bf16[96,3584]{1,0:T(8,128)(2,1)S(1)}, u32[]{:S(2)}, u32[]{:S(2)}) collective-permute-start(bf16[96,3584]{1,0:T(8,128)(2,1)S(1)} %collective-permute-done.9), channel_id=1, source_target_pairs={{0,8},{8,16},{16,24},{24,0},{1,9},{9,17},{17,25},{25,1},{2,10},{10... | collective-permute-start | bytes 2064392 | tf_op jit(solution)/shard_map/ppermute | solution.py:13
  314.0 3.0 copy-start.5
  322.2 177.4 %reduce-scatter.9.cloned.1.call-start = ((), (), s32[]{:S(2)}) async-start(), calls=%async_computation.14 | async-start | bytes 3440640 | tf_op jit(solution)/shard_map/reduce_scatter | solution.py:48
  349.0 66.1 %copy-start.32 = (bf16[1,512,3584]{2,1,0:T(8,128)(2,1)S(1)}, bf16[1,512,3584]{2,1,0:T(8,128)(2,1)}, u32[]{:S(2)}) copy-start(bf16[1,512,3584]{2,1,0:T(8,128)(2,1)} %param.15) | copy-start | bytes 11010052
  349.0 66.1 %copy-start.34 = (f32[384,512]{1,0:T(8,128)S(1)}, f32[384,512]{1,0:T(8,128)}, u32[]{:S(2)}) copy-start(f32[384,512]{1,0:T(8,128)} %copy-done.33) | copy-start | bytes 2359300
  349.0 66.1 %copy-start.37 = (f32[384,512]{1,0:T(8,128)S(1)}, f32[384,512]{1,0:T(8,128)}, u32[]{:S(2)}) copy-start(f32[384,512]{1,0:T(8,128)} %get-tuple-element.17) | copy-start | bytes 2359300
  349.0 26.7 %collective-permute-start.6 = (bf16[96,3584]{1,0:T(8,128)(2,1)S(1)}, bf16[96,3584]{1,0:T(8,128)(2,1)S(1)}, u32[]{:S(2)}, u32[]{:S(2)}) collective-permute-start(bf16[96,3584]{1,0:T(8,128)(2,1)S(1)} %all_to_all.57), channel_id=1, source_target_pairs={{0,8},{8,16},{16,24},{24,0},{1,9},{9,17},{17,25},{25,1},{2,10},{10... | collective-permute-start | bytes 2064392 | tf_op jit(solution)/shard_map/ppermute | solution.py:13
  349.1 40.6 %collective-permute-start.8 = (bf16[96,3584]{1,0:T(8,128)(2,1)S(1)}, bf16[96,3584]{1,0:T(8,128)(2,1)S(1)}, u32[]{:S(2)}, u32[]{:S(2)}) collective-permute-start(bf16[96,3584]{1,0:T(8,128)(2,1)S(1)} %all_to_all.57), channel_id=1, source_target_pairs={{0,24},{8,0},{16,8},{24,16},{1,25},{9,1},{17,9},{25,17},{2,26},{10... | collective-permute-start | bytes 2064392 | tf_op jit(solution)/shard_map/ppermute | solution.py:15
  375.7 28.1 %collective-permute-start.7 = (bf16[96,3584]{1,0:T(8,128)(2,1)S(1)}, bf16[96,3584]{1,0:T(8,128)(2,1)S(1)}, u32[]{:S(2)}, u32[]{:S(2)}) collective-permute-start(bf16[96,3584]{1,0:T(8,128)(2,1)S(1)} %collective-permute-done.6), channel_id=1, source_target_pairs={{0,8},{8,16},{16,24},{24,0},{1,9},{9,17},{17,25},{25,1},{2,10},{10... | collective-permute-start | bytes 2064392 | tf_op jit(solution)/shard_map/ppermute | solution.py:13
  415.1 3.3 copy-start.6
  417.0 3.1 copy-start.20
  417.0 3.1 copy-start.22
  425.8 27.3 %all-to-all-start.1 = ((bf16[8,12,3584]{2,1,0:T(8,128)(2,1)}), bf16[8,12,3584]{2,1,0:T(8,128)(2,1)S(1)}, u32[]{:S(2)}, u32[]{:S(2)}) async-start(bf16[8,12,3584]{2,1,0:T(8,128)(2,1)} %all_to_all.50), calls=%async_computation.2 | async-start | bytes 1835008 | tf_op jit(solution)/shard_map/all_to_all | solution.py:49
  454.0 28.2 %all-to-all-start.3 = ((bf16[8,12,3584]{2,1,0:T(8,128)(2,1)}), bf16[8,12,3584]{2,1,0:T(8,128)(2,1)}, u32[]{:S(2)}, u32[]{:S(2)}) async-start(bf16[8,12,3584]{2,1,0:T(8,128)(2,1)} %all_to_all.54), calls=%async_computation.5 | async-start | bytes 1835008 | tf_op jit(solution)/shard_map/all_to_all | solution.py:49
  458.4 4.1 copy-start.1
  458.4 4.1 copy-start.23
  482.2 28.0 %all-to-all-start.7 = ((bf16[8,12,3584]{2,1,0:T(8,128)(2,1)}), bf16[8,12,3584]{2,1,0:T(8,128)(2,1)}, u32[]{:S(2)}, u32[]{:S(2)}) async-start(bf16[8,12,3584]{2,1,0:T(8,128)(2,1)} %all_to_all.62), calls=%async_computation.11 | async-start | bytes 1835008 | tf_op jit(solution)/shard_map/all_to_all | solution.py:49
  486.5 4.1 copy-start.14
  486.5 4.1 copy-start.27
  490.5 5.0 copy-start.21
  499.6 15.1 %copy-start.16 = (bf16[384,3584]{1,0:T(8,128)(2,1)S(1)}, bf16[384,3584]{1,0:T(8,128)(2,1)}, u32[]{:S(2)}) copy-start(bf16[384,3584]{1,0:T(8,128)(2,1)} %copy-done.15) | copy-start | bytes 8257540
  499.6 15.2 %copy-start.25 = (bf16[384,512]{1,0:T(8,128)(2,1)S(1)}, bf16[384,512]{1,0:T(8,128)(2,1)}, u32[]{:S(2)}) copy-start(bf16[384,512]{1,0:T(8,128)(2,1)} %copy-done.24) | copy-start | bytes 1179652
  510.2 28.3 %all-to-all-start.5 = ((bf16[8,12,3584]{2,1,0:T(8,128)(2,1)}), bf16[8,12,3584]{2,1,0:T(8,128)(2,1)}, u32[]{:S(2)}, u32[]{:S(2)}) async-start(bf16[8,12,3584]{2,1,0:T(8,128)(2,1)} %all_to_all.58), calls=%async_computation.8 | async-start | bytes 1835008 | tf_op jit(solution)/shard_map/all_to_all | solution.py:49
  514.8 7.1 %copy-start.19 = (bf16[8,12,3584]{2,1,0:T(8,128)(2,1)S(1)}, bf16[8,12,3584]{2,1,0:T(8,128)(2,1)}, u32[]{:S(2)}) copy-start(bf16[8,12,3584]{2,1,0:T(8,128)(2,1)} %copy-done.18) | copy-start | bytes 2064388
  (11 other events, 17.6 us)
Sparse Core Ops, SparseCore 0:
  118.7 47.3 reduce-scatter.4
  220.9 47.3 reduce-scatter.6
  322.3 47.2 reduce-scatter.10
  423.8 39.0 reduce-scatter.8
